TPU v7x, 256 devices: a whole 4x4x8 slice. The times are simulated.
256 devices in a mesh: chan: 64 (over z, y_hi, x), seg: 4 (over y_lo, core).
Axes of the slice: x: 4, y: 4 (y_hi: 2, y_lo: 2; y = y_hi * 2 + y_lo), z: 8, core: 2. Of those that a mesh axis runs over, the one named last changes fastest.
Arguments:
- spectra: bfloat16 [32, 128, 2, 8192], P(None, 'seg', None, 'chan'), may hold values from -6 to 6
- plan: int32 [4, 64], replicated, may hold values from 0 to 63, as said below
- assignment: int32 [8192], P('chan'), may hold values from 0 to 8191, as said below
Outputs:
- cross_spectra: float32 [4, 32, 2, 8192, 128], P(None, 'seg', None, 'chan')
Inputs may be any that keep to these rules, and one draw needn't show every extreme that they name: Each row is a pairing of the blocks: plan[r, plan[r, b]] = b and plan[r, b] != b; no two blocks are paired in two different rounds. `assignment`: entries b * 128 to (b + 1) * 128 - 1 are a permutation of that same range of channels.
All inputs are finite; a program needn't handle non-finite values.
Results may differ from a plain program's by a relative error of at most 0.0003.
Values may be sent and summed in bfloat16 or wider, within the bound.
No kernel may reach another device: no remote copies, remote signals or barrier semaphores. Data moves between devices by JAX's collectives and lax.ppermute only.
A program may use at most 128 MiB of HBM per device.

v0:
```python
import math
import jax
import jax.numpy as jnp
from jax import lax
from jax.sharding import PartitionSpec as P


def cross_block(own_rows, other_rows, chan_width):
    real_lhs = own_rows
    imag_lhs = jnp.stack([own_rows[:, :, 1], -own_rows[:, :, 0]], axis=2)
    lhs = jnp.stack([real_lhs, imag_lhs], axis=3)
    return jnp.einsum("fwkci,fwkj->fcij", lhs, other_rows, preferred_element_type=jnp.float32)


def on_device(spectra, plan, assignment):
    bin_count, win_local, _, chan_width = spectra.shape
    seg_count = lax.axis_size("seg")
    group_count = lax.axis_size("chan")
    win_count = win_local * seg_count
    scale = 1.0 / math.sqrt(win_count)
    local_slots = assignment - lax.axis_index("chan") * chan_width
    ordered = jnp.take(spectra, local_slots, axis=3)
    own_rows = lax.all_to_all(ordered, "seg", split_axis=0, concat_axis=1, tiled=True)
    my_bins = own_rows.shape[0]
    piece_rows = my_bins * win_count // group_count
    pieces = own_rows.reshape(group_count, piece_rows, 2 * chan_width)
    held = lax.all_to_all(pieces, "chan", split_axis=0, concat_axis=0, tiled=True)
    round_count = plan.shape[0]
    outgoing = jnp.take(held, plan.T, axis=0)
    arrived = lax.all_to_all(outgoing, "chan", split_axis=0, concat_axis=0, tiled=True)
    results = []
    for round_index in range(round_count):
        other_rows = arrived[:, round_index].reshape(my_bins, win_count, 2, chan_width)
        results.append(cross_block(own_rows, other_rows, chan_width) * scale)
    return jnp.stack(results)


def solution(mesh):
    in_specs = (P(None, "seg", None, "chan"), P(), P("chan"))
    out_specs = P(None, "seg", None, "chan", None)
    return jax.shard_map(
        on_device, mesh=mesh, in_specs=in_specs, out_specs=out_specs, check_vma=False
    )
```

profile of v0, /device:TPU:2, one launch (start us, length us, event | category | flops | bytes accessed | tf_op | source)
XLA Modules:
  0.0 130.8 jit_solution(9304834242603706841)
XLA Ops:
  0.0 0.7 compare_and_fusion.1
  0.7 3.5 %copy.30 = bf16[32,32,2,128]{1,0,2,3:T(8,128)(2,1)S(1)} copy(bf16[32,32,2,128]{3,2,1,0:T(2,128)(2,1)} %param.3) | data formatting | bytes 1048576 | tf_op args[0]
  4.1 2.1 %gather_fusion = bf16[128,32,32,2]{2,1,3,0:T(8,128)(2,1)} fusion(bf16[32,32,2,128]{1,0,2,3:T(8,128)(2,1)S(1)} %copy.30, s32[1024]{0:T(1024)S(1)} %pad_clamp_fusion.1), kind=kCustom, calls=%fused_computation | custom fusion | bytes 1049088 | tf_op jit(solution)/shard_map/jit(_take)/gather | solution.py:22
  6.3 1.9 %select_bitcast_fusion = bf16[32,32,2,128]{1,0,2,3:T(8,128)(2,1)S(1)} fusion(bf16[128,32,32,2]{2,1,3,0:T(8,128)(2,1)} %gather_fusion, pred[128]{0:T(512)(128)(4,1)S(1)} %get-tuple-element.5), kind=kLoop, calls=%fused_computation.3 | loop fusion | flops 262144 | bytes 1048704 | tf_op jit(solution)/shard_map/jit(_take)/select_n | solution.py:22
  8.1 2.1 %copy.31 = bf16[32,32,2,128]{3,1,2,0:T(8,128)(2,1)S(1)} copy(bf16[32,32,2,128]{1,0,2,3:T(8,128)(2,1)S(1)} %select_bitcast_fusion) | data formatting | bytes 1048576 | tf_op jit(solution)/shard_map/jit(_take)/select_n | solution.py:22
  10.2 11.5 %all_to_all.28 = bf16[32,32,2,128]{3,1,2,0:T(8,128)(2,1)S(1)} all-to-all(bf16[32,32,2,128]{3,1,2,0:T(8,128)(2,1)S(1)} %copy.31), channel_id=1, replica_groups=mesh['chan'=64,'seg'=4] {'seg'}, dimensions={0} | all-to-all | bytes 1048576 | tf_op jit(solution)/shard_map/all_to_all | solution.py:23
  21.7 0.5 copy.38
  22.3 1.1 reshape.15
  23.4 14.4 %all-to-all-start.1 = ((bf16[64,16,256]{2,1,0:T(8,128)(2,1)}), bf16[64,16,256]{2,1,0:T(8,128)(2,1)S(1)}, u32[]{:S(2)}, u32[]{:S(2)}) async-start(bf16[64,16,256]{2,1,0:T(8,128)(2,1)} %reshape.15), calls=%async_computation.1 | async-start | bytes 1048576 | tf_op jit(solution)/shard_map/all_to_all | solution.py:27
  37.8 0.1 copy.37
  37.9 0.1 copy.39
  38.0 0.1 reshape.26
  38.2 16.9 %all-to-all-done.1 = bf16[64,16,256]{2,1,0:T(8,128)(2,1)S(1)} async-done(((bf16[64,16,256]{2,1,0:T(8,128)(2,1)}), bf16[64,16,256]{2,1,0:T(8,128)(2,1)S(1)}, u32[]{:S(2)}, u32[]{:S(2)}) %all-to-all-start.1) | async-done | bytes 524320 | tf_op jit(solution)/shard_map/all_to_all | solution.py:27
  55.0 0.8 gather_fusion.1
  55.8 1.5 %broadcast_select_fusion = bf16[64,4,16,256]{3,2,1,0:T(8,128)(2,1)} fusion(bf16[64,4,16,256]{3,2,1,0:T(8,128)(2,1)S(1)} %bitcast.62, pred[64,4]{1,0:T(8,128)(4,1)S(1)} %copy.37), kind=kLoop, calls=%fused_computation.4 | loop fusion | flops 1048576 | bytes 4194560 | tf_op jit(solution)/shard_map/jit(_take)/select_n | solution.py:29
  57.3 7.4 %all-to-all-start.2 = ((bf16[64,4,16,256]{3,2,1,0:T(8,128)(2,1)}), bf16[64,4,16,256]{3,2,1,0:T(8,128)(2,1)S(1)}, u32[]{:S(2)}, u32[]{:S(2)}) async-start(bf16[64,4,16,256]{3,2,1,0:T(8,128)(2,1)} %broadcast_select_fusion), calls=%async_computation.2 | async-start | bytes 4194304 | tf_op jit(solution)/shard_map/all_to_all | solution.py:30
  64.8 1.0 copy.36
  65.9 0.2 copy.60
  66.1 0.2 copy.61
  66.3 0.1 neg.3
  66.3 0.8 maximum_bitcast_fusion
  67.2 47.6 %all-to-all-done.2 = bf16[64,4,16,256]{3,2,1,0:T(8,128)(2,1)S(1)} async-done(((bf16[64,4,16,256]{3,2,1,0:T(8,128)(2,1)}), bf16[64,4,16,256]{3,2,1,0:T(8,128)(2,1)S(1)}, u32[]{:S(2)}, u32[]{:S(2)}) %all-to-all-start.2) | async-done | bytes 2097184 | tf_op jit(solution)/shard_map/all_to_all | solution.py:30
  114.8 1.2 fusion.12
  116.0 2.1 %reshape_squeeze.12 = bf16[8,128,2,128]{3,2,1,0:T(2,128)(2,1)} reshape(bf16[64,1,16,256]{3,2,1,0:T(8,128)(2,1)} %get-tuple-element.7) | data formatting | bytes 1048576 | tf_op jit(solution)/shard_map/reshape;squeeze | solution.py:33
  118.0 2.0 %reshape_squeeze.15 = bf16[8,128,2,128]{3,2,1,0:T(2,128)(2,1)} reshape(bf16[64,1,16,256]{3,2,1,0:T(8,128)(2,1)} %get-tuple-element.8) | data formatting | bytes 1048576 | tf_op jit(solution)/shard_map/reshape;squeeze | solution.py:33
  120.0 1.6 %fusion.1 = f32[1,8,2,128,128]{4,3,2,1,0:T(8,128)S(1)} fusion(bf16[8,128,2,128,1]{3,2,1,0,4:T(2,128)(2,1)} %bitcast.67, bf16[8,128,2,1,128]{1,4,2,3,0:T(8,128)(2,1)S(1)} %copy-done.4, bf16[8,128,2,1,128]{1,4,2,3,0:T(8,128)(2,1)S(1)} %copy-done.1), kind=kOutput, calls=%fused_computation.10 | convolution fusion | flops 135004160 | bytes 2621440 | tf_op jit(solution)/shard_map/fwkci,fwkj->fcij/dot_general | solution.py:12
  121.6 0.4 fusion.7
  122.0 1.0 reshape_squeeze.14
  123.0 2.8 %fusion.5 = f32[1,8,2,128,128]{4,3,2,1,0:T(8,128)} fusion(bf16[8,128,2,128,1]{3,2,1,0,4:T(2,128)(2,1)} %bitcast.70, bf16[8,128,2,1,128]{1,4,2,3,0:T(8,128)(2,1)} %maximum_bitcast_fusion, bf16[8,128,2,1,128]{1,4,2,3,0:T(8,128)(2,1)} %copy.36), kind=kOutput, calls=%fused_computation.14 | convolution fusion | flops 135004160 | bytes 2621440 | tf_op jit(solution)/shard_map/fwkci,fwkj->fcij/dot_general | solution.py:12
  125.8 1.0 reshape_squeeze.13
  126.8 1.7 %fusion.3 = f32[1,8,2,128,128]{4,3,2,1,0:T(8,128)S(1)} fusion(bf16[8,128,2,128,1]{3,2,1,0,4:T(2,128)(2,1)} %bitcast.69, bf16[8,128,2,1,128]{1,4,2,3,0:T(8,128)(2,1)} %maximum_bitcast_fusion, bf16[8,128,2,1,128]{1,4,2,3,0:T(8,128)(2,1)S(1)} %copy-done.3), kind=kOutput, calls=%fused_computation.12 | convolution fusion | flops 135004160 | bytes 2621440 | tf_op jit(solution)/shard_map/fwkci,fwkj->fcij/dot_general | solution.py:12
  128.5 2.3 %pad_maximum_fusion = f32[4,8,2,128,128]{4,3,2,1,0:T(8,128)} fusion(f32[1,8,2,128,128]{4,3,2,1,0:T(8,128)S(1)} %fusion.7, f32[1,8,2,128,128]{4,3,2,1,0:T(8,128)S(1)} %copy-done, f32[1,8,2,128,128]{4,3,2,1,0:T(8,128)S(1)} %fusion.3, f32[1,8,2,128,128]{4,3,2,1,0:T(8,128)S(1)} %fusion.1), kind=kLoop, calls=%fused_computation.2 | loop fusion | flops 3145728 | bytes 8388608 | tf_op jit(solution)/shard_map/stack | solution.py:35
  (22 shorter events, 0.1 us)
Async XLA Ops:
  10.2 27.6 %copy-start.7 = (s32[4,64]{1,0:T(4,128)S(1)}, s32[4,64]{1,0:T(4,128)}, u32[]{:S(2)}) copy-start(s32[4,64]{1,0:T(4,128)} %param.4) | copy-start | bytes 3076
  23.4 31.6 %all-to-all-start.1 = ((bf16[64,16,256]{2,1,0:T(8,128)(2,1)}), bf16[64,16,256]{2,1,0:T(8,128)(2,1)S(1)}, u32[]{:S(2)}, u32[]{:S(2)}) async-start(bf16[64,16,256]{2,1,0:T(8,128)(2,1)} %reshape.15), calls=%async_computation.1 | async-start | bytes 1048576 | tf_op jit(solution)/shard_map/all_to_all | solution.py:27
  57.3 57.4 %all-to-all-start.2 = ((bf16[64,4,16,256]{3,2,1,0:T(8,128)(2,1)}), bf16[64,4,16,256]{3,2,1,0:T(8,128)(2,1)S(1)}, u32[]{:S(2)}, u32[]{:S(2)}) async-start(bf16[64,4,16,256]{3,2,1,0:T(8,128)(2,1)} %broadcast_select_fusion), calls=%async_computation.2 | async-start | bytes 4194304 | tf_op jit(solution)/shard_map/all_to_all | solution.py:30
  116.0 4.0 %copy-start.1 = (bf16[8,128,2,1,128]{1,4,2,3,0:T(8,128)(2,1)S(1)}, bf16[8,128,2,1,128]{1,4,2,3,0:T(8,128)(2,1)}, u32[]{:S(2)}) copy-start(bf16[8,128,2,1,128]{1,4,2,3,0:T(8,128)(2,1)} %copy.36) | copy-start | bytes 1572868
  116.0 4.0 %copy-start.4 = (bf16[8,128,2,1,128]{1,4,2,3,0:T(8,128)(2,1)S(1)}, bf16[8,128,2,1,128]{1,4,2,3,0:T(8,128)(2,1)}, u32[]{:S(2)}) copy-start(bf16[8,128,2,1,128]{1,4,2,3,0:T(8,128)(2,1)} %maximum_bitcast_fusion) | copy-start | bytes 1572868
  120.0 1.6 %copy-start.2 = (bf16[8,128,2,1,128]{1,4,2,3,0:T(8,128)(2,1)S(1)}, bf16[8,128,2,1,128]{1,4,2,3,0:T(8,128)(2,1)}, u32[]{:S(2)}) copy-start(bf16[8,128,2,1,128]{1,4,2,3,0:T(8,128)(2,1)} %copy.36) | copy-start | bytes 1572868
  120.0 1.6 %copy-start.5 = (bf16[8,128,2,1,128]{1,4,2,3,0:T(8,128)(2,1)S(1)}, bf16[8,128,2,1,128]{1,4,2,3,0:T(8,128)(2,1)}, u32[]{:S(2)}) copy-start(bf16[8,128,2,1,128]{1,4,2,3,0:T(8,128)(2,1)} %maximum_bitcast_fusion) | copy-start | bytes 1572868
  120.0 1.6 %copy-start.6 = (bf16[8,128,2,128]{3,2,1,0:T(2,128)(2,1)S(1)}, bf16[8,128,2,128]{3,2,1,0:T(2,128)(2,1)}, u32[]{:S(2)}) copy-start(bf16[8,128,2,128]{3,2,1,0:T(2,128)(2,1)} %reshape_squeeze.15) | copy-start | bytes 1572868
  123.0 3.8 %copy-start.3 = (bf16[8,128,2,1,128]{1,4,2,3,0:T(8,128)(2,1)S(1)}, bf16[8,128,2,1,128]{1,4,2,3,0:T(8,128)(2,1)}, u32[]{:S(2)}) copy-start(bf16[8,128,2,1,128]{1,4,2,3,0:T(8,128)(2,1)} %copy.36) | copy-start | bytes 1572868
  126.8 1.7 %copy-start = (f32[1,8,2,128,128]{4,3,2,1,0:T(8,128)S(1)}, f32[1,8,2,128,128]{4,3,2,1,0:T(8,128)}, u32[]{:S(2)}) copy-start(f32[1,8,2,128,128]{4,3,2,1,0:T(8,128)} %fusion.5) | copy-start | bytes 3145732
where the time goes:
time: 131 us
  waiting for transfers between devices  64.4 us (49%)
  starting transfers between devices  21.8 us (17%)
  local copies, waits for them, and re-layouts  19 us (15%)
  blocking collectives  11.5 us (9%)
  other arithmetic  7.26 us (6%)
  matrix products  6.52 us (5%)
    all_to_all x1, waiting for transfers between devices, on_device(): lax.all_to_all(outgoing, 'chan', split_axis=0, concat_axis=0, tiled=True)  47.6 us
    all_to_all x1, waiting for transfers between devices, on_device(): lax.all_to_all(pieces, 'chan', split_axis=0, concat_axis=0, tiled=True)  16.9 us
    all_to_all x1, starting transfers between devices, on_device(): lax.all_to_all(pieces, 'chan', split_axis=0, concat_axis=0, tiled=True)  14.4 us
    all_to_all x1, blocking collectives, on_device(): lax.all_to_all(ordered, 'seg', split_axis=0, concat_axis=1, tiled=True)  11.5 us
    all_to_all x1, starting transfers between devices, on_device(): lax.all_to_all(outgoing, 'chan', split_axis=0, concat_axis=0, tiled=True)  7.44 us
    dot_general x4, matrix products, cross_block(): jnp.einsum('fwkci,fwkj->fcij', lhs, other_rows, preferred_element_type=jn...  6.52 us
    another operation x4, local copies, waits for them, and re-layouts, on_device(): arrived[:, round_index].reshape(my_bins, win_count, 2, chan_width)  5.92 us
    unnamed x19, local copies, waits for them, and re-layouts  3.86 us
  transfers between devices with their start and end apart: 2, of which 2 were waited for; matrix products, arithmetic and copies ran while one was open for 2% of the time, Pallas kernels for 0%

commit v1 on v0

--- a/solution.py
+++ b/solution.py
@@ -3,6 +3,7 @@
 import jax.numpy as jnp
 from jax import lax
 from jax.sharding import PartitionSpec as P
+from jax.lax import all_to_all, psum
 
 
 def cross_block(own_rows, other_rows, chan_width):
@@ -20,7 +21,9 @@
     scale = 1.0 / math.sqrt(win_count)
     local_slots = assignment - lax.axis_index("chan") * chan_width
     ordered = jnp.take(spectra, local_slots, axis=3)
-    own_rows = lax.all_to_all(ordered, "seg", split_axis=0, concat_axis=1, tiled=True)
+    own_rows = jnp.concatenate(
+        all_to_all(jnp.stack(jnp.split(ordered, psum(1, "seg"), 0), axis=0), "seg", 0, 0), 1
+    )
     my_bins = own_rows.shape[0]
     piece_rows = my_bins * win_count // group_count
     pieces = own_rows.reshape(group_count, piece_rows, 2 * chan_width)

time: 131 us -> 131 us (level)
    another operation x0 -> x6, local copies, waits for them, and re-layouts: none -> 3.28 us  [the longest x5 2.15 us: on_device(): jnp.stack(jnp.split(ordered, psum(1, 'seg'), 0), axis=0)]
    select_n x1 -> x0, local copies, waits for them, and re-layouts: 2.07 us -> none  [on_device(): ordered = jnp.take(spectra, local_slots, axis=3)]
where the time goes in v1:
time: 131 us
  waiting for transfers between devices  64.4 us (49%)
  starting transfers between devices  21.8 us (17%)
  local copies, waits for them, and re-layouts  19.1 us (15%)
  blocking collectives  11.5 us (9%)
  other arithmetic  7.33 us (6%)
  matrix products  6.52 us (5%)
    all_to_all x1, waiting for transfers between devices, on_device(): lax.all_to_all(outgoing, 'chan', split_axis=0, concat_axis=0, tiled=True)  47.6 us
    all_to_all x1, waiting for transfers between devices, on_device(): lax.all_to_all(pieces, 'chan', split_axis=0, concat_axis=0, tiled=True)  16.9 us
    all_to_all x1, starting transfers between devices, on_device(): lax.all_to_all(pieces, 'chan', split_axis=0, concat_axis=0, tiled=True)  14.4 us
    all_to_all x1, blocking collectives, on_device(): all_to_all(jnp.stack(jnp.split(ordered, psum(1, 'seg'), 0), axis=0), 'seg...  11.5 us
    all_to_all x1, starting transfers between devices, on_device(): lax.all_to_all(outgoing, 'chan', split_axis=0, concat_axis=0, tiled=True)  7.44 us
    dot_general x4, matrix products, cross_block(): jnp.einsum('fwkci,fwkj->fcij', lhs, other_rows, preferred_element_type=jn...  6.52 us
    another operation x4, local copies, waits for them, and re-layouts, on_device(): arrived[:, round_index].reshape(my_bins, win_count, 2, chan_width)  5.93 us
    unnamed x19, local copies, waits for them, and re-layouts  3.86 us
  transfers between devices with their start and end apart: 2, of which 2 were waited for; matrix products, arithmetic and copies ran while one was open for 2% of the time, Pallas kernels for 0%

profile of v1, /device:TPU:2, one launch (start us, length us, event | category | flops | bytes accessed | tf_op | source)
XLA Modules:
  0.0 130.9 jit_solution(5096709436907361315)
XLA Ops:
  0.0 0.7 compare_and_fusion.1
  0.7 3.5 %copy.20 = bf16[32,32,2,128]{1,0,2,3:T(8,128)(2,1)S(1)} copy(bf16[32,32,2,128]{3,2,1,0:T(2,128)(2,1)} %param.3) | data formatting | bytes 1048576 | tf_op args[0]
  4.1 2.1 %gather_fusion = bf16[128,32,32,2]{2,1,3,0:T(8,128)(2,1)} fusion(bf16[32,32,2,128]{1,0,2,3:T(8,128)(2,1)S(1)} %copy.20, s32[1024]{0:T(1024)S(1)} %pad_clamp_fusion.1), kind=kCustom, calls=%fused_computation | custom fusion | bytes 1049088 | tf_op jit(solution)/shard_map/jit(_take)/gather | solution.py:23
  6.3 1.9 %select_bitcast_fusion = bf16[32,32,2,128]{1,0,2,3:T(8,128)(2,1)S(1)} fusion(bf16[128,32,32,2]{2,1,3,0:T(8,128)(2,1)} %gather_fusion, pred[128]{0:T(512)(128)(4,1)S(1)} %get-tuple-element.5), kind=kLoop, calls=%fused_computation.3 | loop fusion | flops 262144 | bytes 1048704 | tf_op jit(solution)/shard_map/jit(_take)/select_n | solution.py:23
  8.1 0.4 slice_bitcast_fusion.3
  8.5 0.4 copy.21
  9.0 0.4 copy.24
  9.4 0.4 copy.23
  9.9 0.4 copy.22
  10.4 11.5 %all_to_all.15 = bf16[4,8,32,2,128]{4,2,3,1,0:T(8,128)(2,1)S(1)} all-to-all(bf16[4,8,32,2,128]{4,2,3,1,0:T(8,128)(2,1)S(1)} %pad_maximum_fusion.2), channel_id=1, replica_groups=mesh['chan'=64,'seg'=4] {'seg'}, dimensions={0} | all-to-all | bytes 1048576 | tf_op jit(solution)/shard_map/all_to_all | solution.py:25
  21.9 0.5 copy.30
  22.4 1.1 reshape_reshape.3
  23.5 14.4 %all-to-all-start.1 = ((bf16[64,16,256]{2,1,0:T(8,128)(2,1)}), bf16[64,16,256]{2,1,0:T(8,128)(2,1)S(1)}, u32[]{:S(2)}, u32[]{:S(2)}) async-start(bf16[64,16,256]{2,1,0:T(8,128)(2,1)} %reshape_reshape.3), calls=%async_computation.1 | async-start | bytes 1048576 | tf_op jit(solution)/shard_map/all_to_all | solution.py:30
  38.3 16.9 %all-to-all-done.1 = bf16[64,16,256]{2,1,0:T(8,128)(2,1)S(1)} async-done(((bf16[64,16,256]{2,1,0:T(8,128)(2,1)}), bf16[64,16,256]{2,1,0:T(8,128)(2,1)S(1)}, u32[]{:S(2)}, u32[]{:S(2)}) %all-to-all-start.1) | async-done | bytes 524320 | tf_op jit(solution)/shard_map/all_to_all | solution.py:30
  55.2 0.8 gather_fusion.1
  55.9 1.5 %broadcast_select_fusion = bf16[64,4,16,256]{3,2,1,0:T(8,128)(2,1)} fusion(bf16[64,4,16,256]{3,2,1,0:T(8,128)(2,1)S(1)} %bitcast.71, pred[64,4]{1,0:T(8,128)(4,1)S(1)} %copy.29), kind=kLoop, calls=%fused_computation.4 | loop fusion | flops 1048576 | bytes 4194560 | tf_op jit(solution)/shard_map/jit(_take)/select_n | solution.py:32
  57.5 7.4 %all-to-all-start.2 = ((bf16[64,4,16,256]{3,2,1,0:T(8,128)(2,1)}), bf16[64,4,16,256]{3,2,1,0:T(8,128)(2,1)S(1)}, u32[]{:S(2)}, u32[]{:S(2)}) async-start(bf16[64,4,16,256]{3,2,1,0:T(8,128)(2,1)} %broadcast_select_fusion), calls=%async_computation.2 | async-start | bytes 4194304 | tf_op jit(solution)/shard_map/all_to_all | solution.py:33
  65.0 1.0 copy.28
  66.1 0.2 copy.53
  66.2 0.2 copy.54
  66.5 0.8 maximum_bitcast_fusion
  67.3 47.6 %all-to-all-done.2 = bf16[64,4,16,256]{3,2,1,0:T(8,128)(2,1)S(1)} async-done(((bf16[64,4,16,256]{3,2,1,0:T(8,128)(2,1)}), bf16[64,4,16,256]{3,2,1,0:T(8,128)(2,1)S(1)}, u32[]{:S(2)}, u32[]{:S(2)}) %all-to-all-start.2) | async-done | bytes 2097184 | tf_op jit(solution)/shard_map/all_to_all | solution.py:33
  114.9 1.2 fusion.12
  116.1 2.1 %reshape_squeeze.12 = bf16[8,128,2,128]{3,2,1,0:T(2,128)(2,1)} reshape(bf16[64,1,16,256]{3,2,1,0:T(8,128)(2,1)} %get-tuple-element.7) | data formatting | bytes 1048576 | tf_op jit(solution)/shard_map/reshape;squeeze | solution.py:36
  118.2 2.0 %reshape_squeeze.15 = bf16[8,128,2,128]{3,2,1,0:T(2,128)(2,1)} reshape(bf16[64,1,16,256]{3,2,1,0:T(8,128)(2,1)} %get-tuple-element.8) | data formatting | bytes 1048576 | tf_op jit(solution)/shard_map/reshape;squeeze | solution.py:36
  120.2 1.6 %fusion.1 = f32[1,8,2,128,128]{4,3,2,1,0:T(8,128)S(1)} fusion(bf16[8,128,2,128,1]{3,2,1,0,4:T(2,128)(2,1)} %bitcast.75, bf16[8,128,2,1,128]{1,4,2,3,0:T(8,128)(2,1)S(1)} %copy-done.4, bf16[8,128,2,1,128]{1,4,2,3,0:T(8,128)(2,1)S(1)} %copy-done.1), kind=kOutput, calls=%fused_computation.10 | convolution fusion | flops 135004160 | bytes 2621440 | tf_op jit(solution)/shard_map/fwkci,fwkj->fcij/dot_general | solution.py:13
  121.8 0.4 fusion.7
  122.2 1.0 reshape_squeeze.14
  123.2 2.8 %fusion.5 = f32[1,8,2,128,128]{4,3,2,1,0:T(8,128)} fusion(bf16[8,128,2,128,1]{3,2,1,0,4:T(2,128)(2,1)} %bitcast.78, bf16[8,128,2,1,128]{1,4,2,3,0:T(8,128)(2,1)} %maximum_bitcast_fusion, bf16[8,128,2,1,128]{1,4,2,3,0:T(8,128)(2,1)} %copy.28), kind=kOutput, calls=%fused_computation.14 | convolution fusion | flops 135004160 | bytes 2621440 | tf_op jit(solution)/shard_map/fwkci,fwkj->fcij/dot_general | solution.py:13
  126.0 1.0 reshape_squeeze.13
  126.9 1.7 %fusion.3 = f32[1,8,2,128,128]{4,3,2,1,0:T(8,128)S(1)} fusion(bf16[8,128,2,128,1]{3,2,1,0,4:T(2,128)(2,1)} %bitcast.77, bf16[8,128,2,1,128]{1,4,2,3,0:T(8,128)(2,1)} %maximum_bitcast_fusion, bf16[8,128,2,1,128]{1,4,2,3,0:T(8,128)(2,1)S(1)} %copy-done.3), kind=kOutput, calls=%fused_computation.12 | convolution fusion | flops 135004160 | bytes 2621440 | tf_op jit(solution)/shard_map/fwkci,fwkj->fcij/dot_general | solution.py:13
  128.7 2.3 %pad_maximum_fusion = f32[4,8,2,128,128]{4,3,2,1,0:T(8,128)} fusion(f32[1,8,2,128,128]{4,3,2,1,0:T(8,128)S(1)} %fusion.7, f32[1,8,2,128,128]{4,3,2,1,0:T(8,128)S(1)} %copy-done, f32[1,8,2,128,128]{4,3,2,1,0:T(8,128)S(1)} %fusion.3, f32[1,8,2,128,128]{4,3,2,1,0:T(8,128)S(1)} %fusion.1), kind=kLoop, calls=%fused_computation.2 | loop fusion | flops 3145728 | bytes 8388608 | tf_op jit(solution)/shard_map/stack | solution.py:38
  (27 shorter events, 0.6 us)
Async XLA Ops:
  10.4 27.6 %copy-start.7 = (s32[4,64]{1,0:T(4,128)S(1)}, s32[4,64]{1,0:T(4,128)}, u32[]{:S(2)}) copy-start(s32[4,64]{1,0:T(4,128)} %param.4) | copy-start | bytes 3076
  23.5 31.6 %all-to-all-start.1 = ((bf16[64,16,256]{2,1,0:T(8,128)(2,1)}), bf16[64,16,256]{2,1,0:T(8,128)(2,1)S(1)}, u32[]{:S(2)}, u32[]{:S(2)}) async-start(bf16[64,16,256]{2,1,0:T(8,128)(2,1)} %reshape_reshape.3), calls=%async_computation.1 | async-start | bytes 1048576 | tf_op jit(solution)/shard_map/all_to_all | solution.py:30
  57.5 57.4 %all-to-all-start.2 = ((bf16[64,4,16,256]{3,2,1,0:T(8,128)(2,1)}), bf16[64,4,16,256]{3,2,1,0:T(8,128)(2,1)S(1)}, u32[]{:S(2)}, u32[]{:S(2)}) async-start(bf16[64,4,16,256]{3,2,1,0:T(8,128)(2,1)} %broadcast_select_fusion), calls=%async_computation.2 | async-start | bytes 4194304 | tf_op jit(solution)/shard_map/all_to_all | solution.py:33
  116.1 4.0 %copy-start.1 = (bf16[8,128,2,1,128]{1,4,2,3,0:T(8,128)(2,1)S(1)}, bf16[8,128,2,1,128]{1,4,2,3,0:T(8,128)(2,1)}, u32[]{:S(2)}) copy-start(bf16[8,128,2,1,128]{1,4,2,3,0:T(8,128)(2,1)} %copy.28) | copy-start | bytes 1572868
  116.1 4.0 %copy-start.4 = (bf16[8,128,2,1,128]{1,4,2,3,0:T(8,128)(2,1)S(1)}, bf16[8,128,2,1,128]{1,4,2,3,0:T(8,128)(2,1)}, u32[]{:S(2)}) copy-start(bf16[8,128,2,1,128]{1,4,2,3,0:T(8,128)(2,1)} %maximum_bitcast_fusion) | copy-start | bytes 1572868
  120.1 1.6 %copy-start.2 = (bf16[8,128,2,1,128]{1,4,2,3,0:T(8,128)(2,1)S(1)}, bf16[8,128,2,1,128]{1,4,2,3,0:T(8,128)(2,1)}, u32[]{:S(2)}) copy-start(bf16[8,128,2,1,128]{1,4,2,3,0:T(8,128)(2,1)} %copy.28) | copy-start | bytes 1572868
  120.1 1.6 %copy-start.5 = (bf16[8,128,2,1,128]{1,4,2,3,0:T(8,128)(2,1)S(1)}, bf16[8,128,2,1,128]{1,4,2,3,0:T(8,128)(2,1)}, u32[]{:S(2)}) copy-start(bf16[8,128,2,1,128]{1,4,2,3,0:T(8,128)(2,1)} %maximum_bitcast_fusion) | copy-start | bytes 1572868
  120.1 1.6 %copy-start.6 = (bf16[8,128,2,128]{3,2,1,0:T(2,128)(2,1)S(1)}, bf16[8,128,2,128]{3,2,1,0:T(2,128)(2,1)}, u32[]{:S(2)}) copy-start(bf16[8,128,2,128]{3,2,1,0:T(2,128)(2,1)} %reshape_squeeze.15) | copy-start | bytes 1572868
  123.2 3.8 %copy-start.3 = (bf16[8,128,2,1,128]{1,4,2,3,0:T(8,128)(2,1)S(1)}, bf16[8,128,2,1,128]{1,4,2,3,0:T(8,128)(2,1)}, u32[]{:S(2)}) copy-start(bf16[8,128,2,1,128]{1,4,2,3,0:T(8,128)(2,1)} %copy.28) | copy-start | bytes 1572868
  126.9 1.7 %copy-start = (f32[1,8,2,128,128]{4,3,2,1,0:T(8,128)S(1)}, f32[1,8,2,128,128]{4,3,2,1,0:T(8,128)}, u32[]{:S(2)}) copy-start(f32[1,8,2,128,128]{4,3,2,1,0:T(8,128)} %fusion.5) | copy-start | bytes 3145732
